TPU v7x, 256 devices: a whole 4x4x8 slice. The times are simulated.
256 devices in a mesh: pb: 8 (over y, core), kv: 32 (over z, x).
Axes of the slice: x: 4, y: 4, z: 8, core: 2. Of those that a mesh axis runs over, the one named last changes fastest.
Arguments:
- queries: bfloat16 [65536, 4096], P(('pb', 'kv')), may hold values from -6 to 6
- keys: bfloat16 [8192, 4096], P(('pb', 'kv')), may hold values from -6 to 6
- values: bfloat16 [8192, 4096], P(('pb', 'kv')), may hold values from -6 to 6
- key_lists: int32 [512, 8], P('pb'), may hold values from 0 to 63, as said below
- counts: int32 [512], P('pb'), may hold values from 1 to 8, as said below
Outputs:
- attended: bfloat16 [65536, 4096], P(('pb', 'kv'))
Inputs may be any that keep to these rules, and one draw needn't show every extreme that they name: For every query block the first counts entries of its row of key_lists name different key blocks; entries past counts are valid block numbers that do not take part. `counts`: some query block uses all 8 entries of its list.
All inputs are finite; a program needn't handle non-finite values.
Results may differ from a plain program's by a relative error of at most 0.011.
Values may be sent and summed in bfloat16 or wider, within the bound.
No kernel may reach another device: no remote copies, remote signals or barrier semaphores. Data moves between devices by JAX's collectives and lax.ppermute only.
A program may use at most 64 MiB of HBM per device.

v0:
```python
import math
import jax
import jax.numpy as jnp
from jax import lax
from jax.sharding import PartitionSpec as P

HEADS = 32
HD = 128
BLK = 128
MOST = 8


def regroup(split_array, kv_count, pb_count):
    tokens_each = split_array.shape[0] // (kv_count * pb_count)
    shaped = split_array.reshape(kv_count, pb_count, tokens_each, split_array.shape[1])
    return shaped.transpose(1, 0, 2, 3).reshape(-1, split_array.shape[1])


def per_device(queries, keys, values, key_lists, counts):
    kv_count = lax.axis_size("kv")
    pb_count = lax.axis_size("pb")
    head_local = HEADS // kv_count
    scaling = HD ** (-0.5)
    key_whole, value_whole = (
        lax.all_gather(keys, "pb", axis=0, tiled=True),
        lax.all_gather(values, "pb", axis=0, tiled=True),
    )
    key_split, value_split = (
        lax.all_to_all(key_whole, "kv", split_axis=1, concat_axis=0, tiled=True),
        lax.all_to_all(value_whole, "kv", split_axis=1, concat_axis=0, tiled=True),
    )
    key_heads = regroup(key_split, kv_count, pb_count)
    value_heads = regroup(value_split, kv_count, pb_count)
    key_blocks = key_heads.reshape(-1, BLK, head_local, HD)
    value_blocks = value_heads.reshape(-1, BLK, head_local, HD)
    slot_of_key = jnp.arange(MOST * BLK, dtype=jnp.int32) // BLK

    def padded_group(item):
        group_queries, group_lists, group_counts = item
        members = group_queries.shape[0]
        listed_keys = key_blocks[group_lists].reshape(members, MOST * BLK, head_local, HD)
        listed_values = value_blocks[group_lists].reshape(members, MOST * BLK, head_local, HD)
        scores = (
            jnp.einsum(
                "gqhd,gkhd->ghqk", group_queries, listed_keys, preferred_element_type=jnp.float32
            )
            * scaling
        )
        usable = (slot_of_key[None, :] < group_counts[:, None])[:, None, None, :]
        largest = jnp.max(jnp.where(usable, scores, -jnp.inf), axis=-1, keepdims=True)
        raised = jnp.where(usable, jnp.exp(scores - largest), 0.0)
        totals = jnp.sum(raised, axis=-1, keepdims=True)
        weights = (raised / totals).astype(jnp.bfloat16)
        output = jnp.einsum(
            "ghqk,gkhd->gqhd", weights, listed_values, preferred_element_type=jnp.float32
        )
        return output.astype(jnp.bfloat16)

    query_blocks = queries.reshape(-1, BLK, queries.shape[1])
    exchanged = lax.all_to_all(query_blocks, "kv", split_axis=2, concat_axis=0, tiled=True)
    block_total = exchanged.shape[0]
    rows = exchanged.shape[1]
    per_group = math.gcd(block_total, max(1, 512 // rows))
    group_total = block_total // per_group
    grouped = exchanged.reshape(group_total, per_group, rows, head_local, HD)
    lists_grouped = key_lists.reshape(group_total, per_group, key_lists.shape[1])
    counts_grouped = counts.reshape(group_total, per_group)
    produced = lax.map(padded_group, (grouped, lists_grouped, counts_grouped))
    joined = produced.reshape(block_total, rows, head_local * HD)
    result = lax.all_to_all(joined, "kv", split_axis=0, concat_axis=2, tiled=True)
    return result.reshape(queries.shape)


def solution(mesh):
    return jax.shard_map(
        per_device,
        mesh=mesh,
        in_specs=(
            P(("pb", "kv"), None),
            P(("pb", "kv"), None),
            P(("pb", "kv"), None),
            P("pb", None),
            P("pb"),
        ),
        out_specs=P(("pb", "kv"), None),
        check_vma=False,
    )
```

profile of v0, /device:TPU:2, one launch (start us, length us, event | category | flops | bytes accessed | tf_op | source)
XLA Modules:
  0.0 411.0 jit_solution(12888155072686574849)
XLA Ops:
  6.5 6.2 %copy.31 = bf16[2,128,4096]{1,0,2:T(2,128)(2,1)} copy(bf16[2,128,4096]{2,1,0:T(8,128)(2,1)} %bitcast.84) | data formatting | bytes 4194304 | tf_op jit(solution)/shard_map/reshape | solution.py:59
  12.7 11.6 %all-to-all-start.1 = ((bf16[2,128,4096]{1,0,2:T(2,128)(2,1)}), bf16[2,128,4096]{1,0,2:T(2,128)(2,1)S(1)}, u32[]{:S(2)}, u32[]{:S(2)}) async-start(bf16[2,128,4096]{1,0,2:T(2,128)(2,1)} %copy.31), calls=%async_computation.1 | async-start | bytes 4194304 | tf_op jit(solution)/shard_map/all_to_all | solution.py:60
  25.1 30.8 %all-gather.5.cloned.1.call-done = bf16[256,4096]{1,0:T(8,128)(2,1)} async-done(((bf16[32,4096]{1,0:T(8,128)(2,1)}), bf16[256,4096]{1,0:T(8,128)(2,1)}) %all-gather.5.cloned.1.call-update) | async-done | bytes 2097168 | tf_op jit(solution)/shard_map/all_gather | solution.py:25
  55.9 4.1 copy.34
  60.0 13.6 %all-to-all-done.1 = bf16[2,128,4096]{1,0,2:T(2,128)(2,1)S(1)} async-done(((bf16[2,128,4096]{1,0,2:T(2,128)(2,1)}), bf16[2,128,4096]{1,0,2:T(2,128)(2,1)S(1)}, u32[]{:S(2)}, u32[]{:S(2)}) %all-to-all-start.1) | async-done | bytes 2097184 | tf_op jit(solution)/shard_map/all_to_all | solution.py:60
  73.6 6.9 %all-to-all-start.2 = ((bf16[256,32,128]{0,2,1:T(8,128)(2,1)}), bf16[256,32,128]{0,2,1:T(8,128)(2,1)}, u32[]{:S(2)}, u32[]{:S(2)}) async-start(bf16[256,32,128]{0,2,1:T(8,128)(2,1)} %bitcast.76), calls=%async_computation.2 | async-start | bytes 4194304 | tf_op jit(solution)/shard_map/all_to_all | solution.py:29
  81.2 30.8 %all-gather.3.cloned.1.call-done = bf16[256,4096]{1,0:T(8,128)(2,1)} async-done(((bf16[32,4096]{1,0:T(8,128)(2,1)}), bf16[256,4096]{1,0:T(8,128)(2,1)}) %all-gather.3.cloned.1.call-update) | async-done | bytes 2097168 | tf_op jit(solution)/shard_map/all_gather | solution.py:26
  112.1 4.1 copy.28
  116.1 12.9 %all-to-all-done.2 = bf16[256,32,128]{0,2,1:T(8,128)(2,1)} async-done(((bf16[256,32,128]{0,2,1:T(8,128)(2,1)}), bf16[256,32,128]{0,2,1:T(8,128)(2,1)}, u32[]{:S(2)}, u32[]{:S(2)}) %all-to-all-start.2) | async-done | bytes 2097184 | tf_op jit(solution)/shard_map/all_to_all | solution.py:29
  129.1 6.7 %all-to-all-start = ((bf16[256,32,128]{0,2,1:T(8,128)(2,1)}), bf16[256,32,128]{0,2,1:T(8,128)(2,1)}, u32[]{:S(2)}, u32[]{:S(2)}) async-start(bf16[256,32,128]{0,2,1:T(8,128)(2,1)} %bitcast.77), calls=%async_computation | async-start | bytes 4194304 | tf_op jit(solution)/shard_map/all_to_all | solution.py:30
  137.7 4.1 copy.33
  141.7 4.1 copy.35
  145.8 2.0 copy.36
  147.8 37.0 %all-to-all-done = bf16[256,32,128]{0,2,1:T(8,128)(2,1)} async-done(((bf16[256,32,128]{0,2,1:T(8,128)(2,1)}), bf16[256,32,128]{0,2,1:T(8,128)(2,1)}, u32[]{:S(2)}, u32[]{:S(2)}) %all-to-all-start) | async-done | bytes 2097184 | tf_op jit(solution)/shard_map/all_to_all | solution.py:30
  184.8 4.1 copy.29
  188.9 3.4 copy.30
  192.2 154.8 %while.11 = (s32[]{:T(128)}, bf16[16,4,128,1,128]{4,2,1,0,3:T(8,128)(2,1)}, s32[16,4,8]{2,1,0:T(4,128)S(1)}, bf16[64,128,1,128]{3,1,0,2:T(8,128)(2,1)}, s32[16,4...) while((s32[]{:T(128)}, ...), condition=%wide.region_3.4_spmd.clone, body=%wide.region_0.3_spmd.clone.sunk | while | flops 272709728 | bytes 15493133 | solution.py:68
  194.5 2.0 fusion.36
  196.5 2.3 gather_fusion
  198.9 2.2 fusion.37
  204.2 2.0 fusion.36
  206.2 2.3 gather_fusion
  208.6 2.2 fusion.37
  213.9 2.0 fusion.36
  215.9 2.3 gather_fusion
  218.2 2.2 fusion.37
  223.5 2.0 fusion.36
  225.6 2.3 gather_fusion
  227.9 2.2 fusion.37
  233.2 2.0 fusion.36
  235.2 2.3 gather_fusion
  237.6 2.2 fusion.37
  242.9 2.0 fusion.36
  244.9 2.3 gather_fusion
  247.3 2.2 fusion.37
  252.6 2.0 fusion.36
  254.6 2.3 gather_fusion
  256.9 2.2 fusion.37
  262.2 2.0 fusion.36
  264.3 2.3 gather_fusion
  266.6 2.2 fusion.37
  271.9 2.0 fusion.36
  273.9 2.3 gather_fusion
  276.3 2.2 fusion.37
  281.6 2.0 fusion.36
  283.6 2.3 gather_fusion
  285.9 2.2 fusion.37
  291.3 2.0 fusion.36
  293.3 2.3 gather_fusion
  295.6 2.2 fusion.37
  300.9 2.0 fusion.36
  302.9 2.3 gather_fusion
  305.3 2.2 fusion.37
  310.6 2.0 fusion.36
  312.6 2.3 gather_fusion
  315.0 2.2 fusion.37
  322.3 2.3 gather_fusion
  324.6 2.2 fusion.37
  332.0 2.3 gather_fusion
  334.3 2.2 fusion.37
  341.6 2.3 gather_fusion
  344.0 2.2 fusion.37
  347.0 53.5 %all_to_all.62 = bf16[64,128,128]{2,1,0:T(8,128)(2,1)S(1)} all-to-all(bf16[64,128,128]{2,1,0:T(8,128)(2,1)} %bitcast.85), channel_id=1, replica_groups=mesh['pb'=8,'kv'=32] {'kv'}, dimensions={0} | all-to-all | bytes 4194304 | tf_op jit(solution)/shard_map/all_to_all | solution.py:70
  401.8 2.3 copy.45
  (176 shorter events, 60.0 us)
Async XLA Ops:
  12.7 60.9 %all-to-all-start.1 = ((bf16[2,128,4096]{1,0,2:T(2,128)(2,1)}), bf16[2,128,4096]{1,0,2:T(2,128)(2,1)S(1)}, u32[]{:S(2)}, u32[]{:S(2)}) async-start(bf16[2,128,4096]{1,0,2:T(2,128)(2,1)} %copy.31), calls=%async_computation.1 | async-start | bytes 4194304 | tf_op jit(solution)/shard_map/all_to_all | solution.py:60
  24.3 31.6 %all-gather.5.cloned.1.call-start = ((), (), s32[]{:S(2)}) async-start(), calls=%async_computation.5 | async-start | bytes 2359296 | tf_op jit(solution)/shard_map/all_gather | solution.py:25
  73.6 55.5 %all-to-all-start.2 = ((bf16[256,32,128]{0,2,1:T(8,128)(2,1)}), bf16[256,32,128]{0,2,1:T(8,128)(2,1)}, u32[]{:S(2)}, u32[]{:S(2)}) async-start(bf16[256,32,128]{0,2,1:T(8,128)(2,1)} %bitcast.76), calls=%async_computation.2 | async-start | bytes 4194304 | tf_op jit(solution)/shard_map/all_to_all | solution.py:29
  80.5 31.6 %all-gather.3.cloned.1.call-start = ((), (), s32[]{:S(2)}) async-start(), calls=%async_computation.4 | async-start | bytes 2359296 | tf_op jit(solution)/shard_map/all_gather | solution.py:26
  129.1 6.8 %copy-start = (s32[64,8]{0,1:T(8,128)S(1)}, s32[64,8]{0,1:T(8,128)}, u32[]{:S(2)}) copy-start(s32[64,8]{0,1:T(8,128)} %param.10) | copy-start | bytes 6148
  129.1 6.9 %copy-start.1 = (s32[64]{0:T(128)S(1)}, s32[64]{0:T(128)}, u32[]{:S(2)}) copy-start(s32[64]{0:T(128)} %param.11) | copy-start | bytes 772
  129.1 55.7 %all-to-all-start = ((bf16[256,32,128]{0,2,1:T(8,128)(2,1)}), bf16[256,32,128]{0,2,1:T(8,128)(2,1)}, u32[]{:S(2)}, u32[]{:S(2)}) async-start(bf16[256,32,128]{0,2,1:T(8,128)(2,1)} %bitcast.77), calls=%async_computation | async-start | bytes 4194304 | tf_op jit(solution)/shard_map/all_to_all | solution.py:30
Sparse Core Ops, SparseCore 0:
  27.0 28.8 all-gather.4
  83.2 28.8 all-gather.2
where the time goes:
time: 413 us; the launch traced here: 411 us
  waiting for transfers between devices  127 us (31%)
  local copies, waits for them, and re-layouts  101 us (24%)
  matrix products  56.6 us (14%)
  blocking collectives  53.5 us (13%)
  other arithmetic  33.6 us (8%)
  starting transfers between devices  25.4 us (6%)
  between operations  13.5 us (3%)
    all_to_all x1, blocking collectives, per_device(): lax.all_to_all(joined, 'kv', split_axis=0, concat_axis=2, tiled=True)  53.5 us
    gather x16, local copies, waits for them, and re-layouts, padded_group(): value_blocks[group_lists].reshape(members, MOST * BLK, head_local, HD)  37.4 us
    all_to_all x1, waiting for transfers between devices, per_device(): lax.all_to_all(value_whole, 'kv', split_axis=1, concat_axis=0, tiled=True)  37 us
    dot_general x16, matrix products, padded_group(): jnp.einsum('ghqk,gkhd->gqhd', weights, listed_values, preferred_element_t...  35.1 us
    sub x16, other arithmetic, padded_group(): raised = jnp.where(usable, jnp.exp(scores - largest), 0.0)  32.1 us
    all_gather x1, waiting for transfers between devices, per_device(): lax.all_gather(keys, 'pb', axis=0, tiled=True)  30.8 us
    all_gather x1, waiting for transfers between devices, per_device(): lax.all_gather(values, 'pb', axis=0, tiled=True)  30.8 us
    dot_general x16, matrix products, padded_group(): jnp.einsum('gqhd,gkhd->ghqk', group_queries, listed_keys, preferred_eleme...  21.5 us
  transfers between devices with their start and end apart: 5, of which 5 were waited for; matrix products, arithmetic and copies ran while one was open for 5% of the time, Pallas kernels for 0%

commit v1 on v0

--- a/solution.py
+++ b/solution.py
@@ -8,6 +8,13 @@
 HD = 128
 BLK = 128
 MOST = 8
+
+
+def map_masks(vec):
+    mat_out = lax.axis_size("kv")
+    known = jnp.stack(jnp.split(vec, mat_out, 1), 0)
+    far_arr = jnp.concatenate(lax.all_to_all(known, "kv", 0, 0), 0)
+    return far_arr
 
 
 def regroup(split_array, kv_count, pb_count):
@@ -26,7 +33,7 @@
         lax.all_gather(values, "pb", axis=0, tiled=True),
     )
     key_split, value_split = (
-        lax.all_to_all(key_whole, "kv", split_axis=1, concat_axis=0, tiled=True),
+        map_masks(key_whole),
         lax.all_to_all(value_whole, "kv", split_axis=1, concat_axis=0, tiled=True),
     )
     key_heads = regroup(key_split, kv_count, pb_count)

time: 413 us -> 435 us (1.053)
  local copies, waits for them, and re-layouts: 101 us -> 140 us
  waiting for transfers between devices: 127 us -> 103 us
    unnamed x6 -> x37, local copies, waits for them, and re-layouts: 2.39 us -> 47.9 us
    all_gather x1, waiting for transfers between devices: 30.8 us -> 14.9 us  [per_device(): lax.all_gather(keys, 'pb', axis=0, tiled=True)]
    all_to_all x1, waiting for transfers between devices: 13.6 us -> 0.01 us  [per_device(): lax.all_to_all(query_blocks, 'kv', split_axis=2, concat_axis=0, tiled=True)]
    all_to_all x1, waiting for transfers between devices: 37 us -> 41.4 us  [per_device(): lax.all_to_all(value_whole, 'kv', split_axis=1, concat_axis=0, tiled=True)]
  transfers between devices with their start and end apart: 5 -> 5, of which waited for: 5 -> 4; matrix products, arithmetic and copies ran while one was open for 5% -> 15% of each run, Pallas kernels for 0% -> 0%
where the time goes in v1:
time: 435 us; the launch traced here: 432 us
  local copies, waits for them, and re-layouts  140 us (32%)
  waiting for transfers between devices  103 us (24%)
  matrix products  56.6 us (13%)
  blocking collectives  56.4 us (13%)
  other arithmetic  33.7 us (8%)
  starting transfers between devices  28.3 us (7%)
  between operations  13.5 us (3%)
    all_to_all x1, blocking collectives, per_device(): lax.all_to_all(joined, 'kv', split_axis=0, concat_axis=2, tiled=True)  56.4 us
    unnamed x37, local copies, waits for them, and re-layouts  47.9 us
    all_to_all x1, waiting for transfers between devices, per_device(): lax.all_to_all(value_whole, 'kv', split_axis=1, concat_axis=0, tiled=True)  41.4 us
    gather x16, local copies, waits for them, and re-layouts, padded_group(): value_blocks[group_lists].reshape(members, MOST * BLK, head_local, HD)  37.4 us
    dot_general x16, matrix products, padded_group(): jnp.einsum('ghqk,gkhd->gqhd', weights, listed_values, preferred_element_t...  35.1 us
    sub x16, other arithmetic, padded_group(): raised = jnp.where(usable, jnp.exp(scores - largest), 0.0)  32.2 us
    all_gather x1, waiting for transfers between devices, per_device(): lax.all_gather(values, 'pb', axis=0, tiled=True)  29.7 us
    dot_general x16, matrix products, padded_group(): jnp.einsum('gqhd,gkhd->ghqk', group_queries, listed_keys, preferred_eleme...  21.4 us
  transfers between devices with their start and end apart: 5, of which 4 were waited for; matrix products, arithmetic and copies ran while one was open for 15% of the time, Pallas kernels for 0%

profile of v1, /device:TPU:2, one launch (start us, length us, event | category | flops | bytes accessed | tf_op | source)
XLA Modules:
  0.0 431.8 jit_solution(7831437858280431170)
XLA Ops:
  7.3 6.2 %copy.29 = bf16[2,128,4096]{1,0,2:T(2,128)(2,1)} copy(bf16[2,128,4096]{2,1,0:T(8,128)(2,1)} %bitcast.208) | data formatting | bytes 4194304 | tf_op jit(solution)/shard_map/reshape | solution.py:66
  13.4 11.6 %all-to-all-start.1 = ((bf16[2,128,4096]{1,0,2:T(2,128)(2,1)}), bf16[2,128,4096]{1,0,2:T(2,128)(2,1)S(1)}, u32[]{:S(2)}, u32[]{:S(2)}) async-start(bf16[2,128,4096]{1,0,2:T(2,128)(2,1)} %copy.29), calls=%async_computation.1 | async-start | bytes 4194304 | tf_op jit(solution)/shard_map/all_to_all | solution.py:67
  25.0 14.9 %all-gather.5.cloned.1.call-done = bf16[256,4096]{1,0:T(8,128)(2,1)} async-done(((bf16[32,4096]{1,0:T(8,128)(2,1)}), bf16[256,4096]{1,0:T(8,128)(2,1)}) %all-gather.5.cloned.1.call-update) | async-done | bytes 2097168 | tf_op jit(solution)/shard_map/all_gather | solution.py:32
  86.9 10.2 %all-to-all-start.2 = ((bf16[32,256,128]{2,1,0:T(8,128)(2,1)}), bf16[32,256,128]{2,1,0:T(8,128)(2,1)}, u32[]{:S(2)}, u32[]{:S(2)}) async-start(bf16[32,256,128]{2,1,0:T(8,128)(2,1)} %constant_dynamic-update-slice_fusion.1), calls=%async_computation.2 | async-start | bytes 4194304 | tf_op jit(solution)/shard_map/all_to_all | solution.py:16
  97.9 29.7 %all-gather.3.cloned.1.call-done = bf16[256,4096]{1,0:T(8,128)(2,1)} async-done(((bf16[32,4096]{1,0:T(8,128)(2,1)}), bf16[256,4096]{1,0:T(8,128)(2,1)}) %all-gather.3.cloned.1.call-update) | async-done | bytes 2097168 | tf_op jit(solution)/shard_map/all_gather | solution.py:33
  127.6 4.1 copy.26
  131.6 15.2 %all-to-all-done.2 = bf16[32,256,128]{2,1,0:T(8,128)(2,1)} async-done(((bf16[32,256,128]{2,1,0:T(8,128)(2,1)}), bf16[32,256,128]{2,1,0:T(8,128)(2,1)}, u32[]{:S(2)}, u32[]{:S(2)}) %all-to-all-start.2) | async-done | bytes 2097184 | tf_op jit(solution)/shard_map/all_to_all | solution.py:16
  146.8 6.5 %all-to-all-start = ((bf16[256,32,128]{0,2,1:T(8,128)(2,1)}), bf16[256,32,128]{0,2,1:T(8,128)(2,1)}, u32[]{:S(2)}, u32[]{:S(2)}) async-start(bf16[256,32,128]{0,2,1:T(8,128)(2,1)} %bitcast.202), calls=%async_computation | async-start | bytes 4194304 | tf_op jit(solution)/shard_map/all_to_all | solution.py:37
  155.2 4.1 copy.31
  159.2 2.0 copy.32
  161.3 41.4 %all-to-all-done = bf16[256,32,128]{0,2,1:T(8,128)(2,1)} async-done(((bf16[256,32,128]{0,2,1:T(8,128)(2,1)}), bf16[256,32,128]{0,2,1:T(8,128)(2,1)}, u32[]{:S(2)}, u32[]{:S(2)}) %all-to-all-start) | async-done | bytes 2097184 | tf_op jit(solution)/shard_map/all_to_all | solution.py:37
  202.7 4.1 copy.27
  206.7 3.4 copy.28
  210.1 154.8 %while.11 = (s32[]{:T(128)}, bf16[16,4,128,1,128]{4,2,1,0,3:T(8,128)(2,1)}, s32[16,4,8]{2,1,0:T(4,128)S(1)}, bf16[64,128,1,128]{3,1,0,2:T(8,128)(2,1)}, s32[16,4...) while((s32[]{:T(128)}, ...), condition=%wide.region_3.4_spmd.clone, body=%wide.region_0.3_spmd.clone.sunk | while | flops 272709728 | bytes 15493133 | solution.py:75
  212.4 2.0 fusion.36
  214.4 2.3 gather_fusion
  216.8 2.2 fusion.37
  222.1 2.0 fusion.36
  224.1 2.3 gather_fusion
  226.4 2.2 fusion.37
  231.8 2.0 fusion.36
  233.8 2.3 gather_fusion
  236.1 2.2 fusion.37
  241.4 2.0 fusion.36
  243.4 2.3 gather_fusion
  245.8 2.2 fusion.37
  251.1 2.0 fusion.36
  253.1 2.3 gather_fusion
  255.5 2.2 fusion.37
  260.8 2.0 fusion.36
  262.8 2.3 gather_fusion
  265.1 2.2 fusion.37
  270.5 2.0 fusion.36
  272.5 2.3 gather_fusion
  274.8 2.2 fusion.37
  280.1 2.0 fusion.36
  282.1 2.3 gather_fusion
  284.5 2.2 fusion.37
  289.8 2.0 fusion.36
  291.8 2.3 gather_fusion
  294.2 2.2 fusion.37
  299.5 2.0 fusion.36
  301.5 2.3 gather_fusion
  303.8 2.2 fusion.37
  309.2 2.0 fusion.36
  311.2 2.3 gather_fusion
  313.5 2.2 fusion.37
  318.8 2.0 fusion.36
  320.8 2.3 gather_fusion
  323.2 2.2 fusion.37
  328.5 2.0 fusion.36
  330.5 2.3 gather_fusion
  332.9 2.2 fusion.37
  338.2 2.0 fusion.36
  340.2 2.3 gather_fusion
  342.5 2.2 fusion.37
  347.9 2.0 fusion.36
  349.9 2.3 gather_fusion
  352.2 2.2 fusion.37
  357.5 2.0 fusion.36
  359.5 2.3 gather_fusion
  361.9 2.2 fusion.37
  364.9 56.4 %all_to_all.51 = bf16[64,128,128]{2,1,0:T(8,128)(2,1)S(1)} all-to-all(bf16[64,128,128]{2,1,0:T(8,128)(2,1)} %bitcast.209), channel_id=1, replica_groups=mesh['pb'=8,'kv'=32] {'kv'}, dimensions={0} | all-to-all | bytes 4194304 | tf_op jit(solution)/shard_map/all_to_all | solution.py:77
  422.7 2.3 copy.41
  (206 shorter events, 100.9 us)
Async XLA Ops:
  6.5 33.4 %all-gather.5.cloned.1.call-start = ((), (), s32[]{:S(2)}) async-start(), calls=%async_computation.5 | async-start | bytes 2359296 | tf_op jit(solution)/shard_map/all_gather | solution.py:32
  13.4 73.5 %all-to-all-start.1 = ((bf16[2,128,4096]{1,0,2:T(2,128)(2,1)}), bf16[2,128,4096]{1,0,2:T(2,128)(2,1)S(1)}, u32[]{:S(2)}, u32[]{:S(2)}) async-start(bf16[2,128,4096]{1,0,2:T(2,128)(2,1)} %copy.29), calls=%async_computation.1 | async-start | bytes 4194304 | tf_op jit(solution)/shard_map/all_to_all | solution.py:67
  86.9 59.9 %all-to-all-start.2 = ((bf16[32,256,128]{2,1,0:T(8,128)(2,1)}), bf16[32,256,128]{2,1,0:T(8,128)(2,1)}, u32[]{:S(2)}, u32[]{:S(2)}) async-start(bf16[32,256,128]{2,1,0:T(8,128)(2,1)} %constant_dynamic-update-slice_fusion.1), calls=%async_computation.2 | async-start | bytes 4194304 | tf_op jit(solution)/shard_map/all_to_all | solution.py:16
  97.1 30.4 %all-gather.3.cloned.1.call-start = ((), (), s32[]{:S(2)}) async-start(), calls=%async_computation.4 | async-start | bytes 2359296 | tf_op jit(solution)/shard_map/all_gather | solution.py:33
  146.8 6.5 %copy-start = (s32[64,8]{0,1:T(8,128)S(1)}, s32[64,8]{0,1:T(8,128)}, u32[]{:S(2)}) copy-start(s32[64,8]{0,1:T(8,128)} %param.10) | copy-start | bytes 6148
  146.8 6.6 %copy-start.1 = (s32[64]{0:T(128)S(1)}, s32[64]{0:T(128)}, u32[]{:S(2)}) copy-start(s32[64]{0:T(128)} %param.11) | copy-start | bytes 772
  146.8 55.8 %all-to-all-start = ((bf16[256,32,128]{0,2,1:T(8,128)(2,1)}), bf16[256,32,128]{0,2,1:T(8,128)(2,1)}, u32[]{:S(2)}, u32[]{:S(2)}) async-start(bf16[256,32,128]{0,2,1:T(8,128)(2,1)} %bitcast.202), calls=%async_computation | async-start | bytes 4194304 | tf_op jit(solution)/shard_map/all_to_all | solution.py:37
Sparse Core Ops, SparseCore 0:
  9.2 30.6 all-gather.4
  99.9 27.6 all-gather.2
